TPU v7x, 512 devices: a whole 4x8x8 slice. The times are simulated.
512 devices in a mesh: seq: 64 (over y, x, core), ch: 8 (over z).
Axes of the slice: x: 4, y: 8, z: 8, core: 2. Of those that a mesh axis runs over, the one named last changes fastest.
Arguments:
- signal: bfloat16 [1536, 32768], P('ch', 'seq'), may hold values from -16 to 16
- input_norm_gain: float32 [1536], P('ch'), may hold values from 0.25 to 1.75
- value_weight: bfloat16 [1536, 1536], P('seq', 'ch'), may hold values from -0.15625 to 0.15625
- gate_weight: bfloat16 [1536, 1536], P('seq', 'ch'), may hold values from -0.15625 to 0.15625
- depth_taps: float32 [31, 1536], P(None, 'ch'), may hold values from -1 to 1
- cotangent: bfloat16 [1536, 32768], P('ch', 'seq'), may hold values from -6 to 6
Outputs:
- output: bfloat16 [1536, 32768], P('ch', 'seq')
- signal_gradient: bfloat16 [1536, 32768], P('ch', 'seq')
- grad_value: float32 [1536, 1536], P('seq', 'ch')
- grad_gate: float32 [1536, 1536], P('seq', 'ch')
- grad_taps: float32 [31, 1536], P(None, 'ch')
- gain_gradient: float32 [1536], P('ch')
All inputs are finite; a program needn't handle non-finite values.
Results may differ from a plain program's by a relative error of at most 0.02.
Values may be sent and summed in bfloat16 or wider, within the bound.
No kernel may reach another device: no remote copies, remote signals or barrier semaphores. Data moves between devices by JAX's collectives and lax.ppermute only.
A program may use at most 64 MiB of HBM per device.

v0:
```python
import jax
import jax.numpy as jnp
from jax import lax
from jax.sharding import PartitionSpec as P


def extended(cells, sides, width):
    for axis, dim in sides:
        count = lax.axis_size(axis)
        ends = count - 1
        head = lax.slice_in_dim(cells, 0, width, axis=dim)
        tail = lax.slice_in_dim(cells, cells.shape[dim] - width, cells.shape[dim], axis=dim)
        cells = jnp.concatenate(
            [
                lax.ppermute(tail, axis, [(i, (i + 1) % count) for i in range(ends)]),
                cells,
                lax.ppermute(head, axis, [((i + 1) % count, i) for i in range(ends)]),
            ],
            axis=dim,
        )
    return cells


def standardize_rows(columns_in):
    values = columns_in.astype(jnp.float32)
    average = jnp.mean(values, 0, keepdims=True)
    centred = values - average
    spread = jnp.mean(centred * centred, 0, keepdims=True)
    inverse_deviation = lax.rsqrt(spread + 1e-05)
    return (centred * inverse_deviation, inverse_deviation)


def depthwise(padded, kernel):
    channels = padded.shape[0]
    result = lax.conv_general_dilated(
        padded[None],
        kernel,
        (1,),
        "VALID",
        dimension_numbers=("NCH", "OIH", "NCH"),
        feature_group_count=channels,
        precision=lax.Precision.HIGHEST,
    )
    return result[0]


def shards(signal, input_norm_gain, value_weight, gate_weight, depth_taps, cotangent):
    local_cols = signal.shape[0]
    frames = signal.shape[1]
    groups = lax.axis_size("ch")
    block_of_rows = frames // groups
    channel_position = lax.axis_index("ch")
    reach = depth_taps.shape[0] // 2
    complete_signal, complete_gain = (
        lax.all_gather(signal, "ch", axis=0, tiled=True),
        lax.all_gather(input_norm_gain.astype(jnp.bfloat16), "ch", axis=0, tiled=True).astype(
            input_norm_gain.dtype
        ),
    )
    centered_unit, inverse_deviation = standardize_rows(complete_signal)
    normalized_signal = (centered_unit * complete_gain[:, None]).astype(jnp.bfloat16)
    centered_unit_rows = lax.dynamic_slice_in_dim(
        centered_unit, channel_position * block_of_rows, block_of_rows, 1
    )
    row_inverse_deviation = lax.dynamic_slice_in_dim(
        inverse_deviation, channel_position * block_of_rows, block_of_rows, 1
    )
    stacked = jnp.concatenate([value_weight, gate_weight], 1)
    gathered = lax.all_gather(stacked, "seq", axis=0, tiled=True)
    mixed = lax.dot_general(
        gathered, normalized_signal, (((0,), (0,)), ((), ())), preferred_element_type=jnp.float32
    )
    value = mixed[:local_cols]
    gate = mixed[local_cols:]
    sig_gate = jax.nn.sigmoid(gate)
    glued = (value * sig_gate).astype(jnp.bfloat16)
    glued_pad = extended(glued, (("seq", 1),), reach).astype(jnp.float32)
    forward_kernel = depth_taps.T[:, None, :]
    pre = depthwise(glued_pad, forward_kernel)
    sig_pre = jax.nn.sigmoid(pre)
    output = (pre * sig_pre).astype(jnp.bfloat16)
    grad_pre = (cotangent.astype(jnp.float32) * sig_pre * (1.0 + pre * (1.0 - sig_pre))).astype(
        jnp.bfloat16
    )
    grad_pre_f = grad_pre.astype(jnp.float32)
    grad_pad = extended(grad_pre, (("seq", 1),), reach).astype(jnp.float32)
    grad_glued = depthwise(grad_pad, forward_kernel[:, :, ::-1])
    tap_partial = depthwise(glued_pad, grad_pre_f[:, None, :]).T
    grad_taps = lax.psum(tap_partial, "seq")
    grad_v = (grad_glued * sig_gate).astype(jnp.bfloat16)
    grad_g = (grad_glued * value * sig_gate * (1.0 - sig_gate)).astype(jnp.bfloat16)
    grad_both = jnp.concatenate([grad_v, grad_g], 0)
    weight_sums = lax.psum_scatter(
        lax.dot_general(
            normalized_signal,
            grad_both,
            (((1,), (1,)), ((), ())),
            preferred_element_type=jnp.float32,
        ),
        "seq",
        scatter_dimension=0,
        tiled=True,
    )
    grad_value = weight_sums[:, :local_cols]
    grad_gate = weight_sums[:, local_cols:]
    normed_term = jnp.dot(gathered, grad_both, preferred_element_type=jnp.float32)
    normalized_gradient = lax.psum_scatter(
        normed_term.astype(jnp.bfloat16), "ch", scatter_dimension=1, tiled=True
    ).astype(jnp.float32)
    scaled_signal = normalized_gradient * complete_gain[:, None]
    first_moment = jnp.mean(scaled_signal, 0, keepdims=True)
    second_moment = jnp.mean(scaled_signal * centered_unit_rows, 0, keepdims=True)
    gradient_rows = (
        row_inverse_deviation * (scaled_signal - first_moment - centered_unit_rows * second_moment)
    ).astype(jnp.bfloat16)
    signal_gradient = lax.all_to_all(gradient_rows, "ch", split_axis=0, concat_axis=1, tiled=True)
    gain_portion = jnp.sum(normalized_gradient * centered_unit_rows, 1)
    gain_whole = lax.psum(gain_portion, ("seq", "ch"))
    gain_gradient = lax.dynamic_slice_in_dim(
        gain_whole, channel_position * local_cols, local_cols, 0
    )
    return (output, signal_gradient, grad_value, grad_gate, grad_taps, gain_gradient)


def solution(mesh):
    placed = (
        P("ch", "seq"),
        P("ch"),
        P("seq", "ch"),
        P("seq", "ch"),
        P(None, "ch"),
        P("ch", "seq"),
    )
    return jax.shard_map(
        shards,
        mesh=mesh,
        in_specs=placed,
        out_specs=(
            P("ch", "seq"),
            P("ch", "seq"),
            P("seq", "ch"),
            P("seq", "ch"),
            P(None, "ch"),
            P("ch"),
        ),
        check_vma=False,
    )
```

profile of v0, /device:TPU:1, one launch (start us, length us, event | category | flops | bytes accessed | tf_op | source)
XLA Modules:
  0.0 592.0 jit_solution(6644750311934210366)
XLA Ops:
  7.2 0.7 all-gather.5.cloned.1.call-update
  8.0 1.4 pad_maximum_fusion.4
  9.5 0.7 convert_element_type.43
  10.1 1.3 dynamic-slice.4
  12.1 0.2 dynamic-update-slice
  12.3 20.2 %all-reduce = bf16[1536]{0:T(1024)(128)(2,1)S(1)} all-reduce(bf16[1536]{0:T(1024)(128)(2,1)S(1)} %dynamic-update-slice), channel_id=1, replica_groups=mesh['seq'=64,'ch'=8] {'ch'}, use_global_device_ids=true, to_apply=%add | all-reduce | flops 1536 | bytes 6144
  32.6 22.6 %all-gather.5.cloned.1.call-done = bf16[1536,512]{1,0:T(8,128)(2,1)} async-done(((bf16[192,512]{1,0:T(8,128)(2,1)}), bf16[1536,512]{1,0:T(8,128)(2,1)}) %all-gather.5.cloned.1.call-update) | async-done | bytes 1572880 | tf_op jit(solution)/shard_map/all_gather | solution.py:55
  55.2 1.7 copy.41
  56.9 0.3 convert_reduce_fusion
  57.2 0.5 fusion.2
  57.8 85.3 %all-gather.3.cloned.1.call-done = bf16[1536,384]{1,0:T(8,128)(2,1)} async-done(((bf16[24,384]{1,0:T(8,128)(2,1)}), bf16[1536,384]{1,0:T(8,128)(2,1)}) %all-gather.3.cloned.1.call-update) | async-done | bytes 1179664 | tf_op jit(solution)/shard_map/all_gather | solution.py:69
  143.1 2.2 fusion.6
  145.6 2.1 collective-permute-start.1
  147.7 3.4 collective-permute-start
  151.2 1.1 collective-permute-done
  152.3 0.8 fusion.33
  153.2 0.4 reshape.83
  153.6 0.4 copy.44
  154.1 2.0 convolution_select_fusion.1
  156.1 1.4 copy.58
  157.5 1.0 reshape.80
  158.5 2.0 multiply_convert_fusion.5
  160.6 1.9 collective-permute-start.3
  162.5 4.2 collective-permute-start.2
  166.8 1.1 collective-permute-done.2
  168.1 0.4 reshape.84
  168.5 0.4 copy.50
  168.9 2.0 convolution_select_fusion
  171.0 1.4 copy.59
  172.4 1.0 reshape.81
  173.4 1.2 multiply_convert_fusion.4
  174.6 3.5 convolution_convert_fusion
  178.4 1.3 dynamic-slice.5
  180.4 2.1 fusion
  182.4 0.9 copy.55
  183.3 0.4 copy.56
  183.8 2.7 fusion.5
  186.5 38.9 %reduce-scatter.2.cloned.1.call-done = bf16[1536,64]{0,1:T(8,128)(2,1)} async-done(((bf16[1536,512]{0,1:T(8,128)(2,1)}), bf16[1536,64]{0,1:T(8,128)(2,1)}) %reduce-scatter.2.cloned.1.call-update) | async-done | bytes 196624 | tf_op jit(solution)/shard_map/reduce_scatter | solution.py:107
  225.4 1.3 fusion.26
  226.7 1.2 fusion.24
  228.2 0.7 copy.54
  228.9 4.7 all-to-all-start
  233.6 2.2 fusion.49
  235.9 245.9 %psum.14 = f32[31,192]{1,0:T(8,128)} all-reduce(f32[31,192]{1,0:T(8,128)S(1)} %bitcast.60), channel_id=1, replica_groups=mesh['seq'=64,'ch'=8] {'seq'}, use_global_device_ids=true, to_apply=%region_6.0 | all-reduce | flops 5952 | bytes 47616 | tf_op jit(solution)/shard_map/psum | solution.py:89
  481.8 1.5 fusion.46
  483.3 100.8 %psum.15 = f32[1536]{0:T(1024)S(1)} all-reduce(f32[1536]{0:T(1024)S(1)} %get-tuple-element.18), channel_id=1, replica_groups=mesh['seq'=64,'ch'=8] {'seq','ch'}, use_global_device_ids=true, to_apply=%region_8.0 | all-reduce | flops 1536 | bytes 12288 | tf_op jit(solution)/shard_map/psum | solution.py:118
  584.1 0.6 dynamic_slice.8
  584.7 0.8 copy.57
  (33 shorter events, 1.3 us)
Async XLA Ops:
  7.2 146.9 %copy-start = (f32[31,192]{1,0:T(8,128)S(1)}, f32[31,192]{1,0:T(8,128)}, u32[]{:S(2)}) copy-start(f32[31,192]{1,0:T(8,128)} %param.10) | copy-start | bytes 71428
  7.2 48.0 %all-gather.5.cloned.1.call-start = ((), (), s32[]{:S(2)}) async-start(), calls=%async_computation.3 | async-start | bytes 1769472 | tf_op jit(solution)/shard_map/all_gather | solution.py:55
  7.9 135.2 %all-gather.3.cloned.1.call-start = ((), (), s32[]{:S(2)}) async-start(), calls=%async_computation.2 | async-start | bytes 1198080 | tf_op jit(solution)/shard_map/all_gather | solution.py:69
  9.4 216.0 %reduce-scatter.2.cloned.1.call-start = ((), (), s32[]{:S(2)}) async-start(), calls=%async_computation.4 | async-start | bytes 1769472 | tf_op jit(solution)/shard_map/reduce_scatter | solution.py:107
  145.3 8.7 %copy-start.2 = (pred[8,68]{0,1:T(8,128)(4,1)S(1)}, pred[8,68]{0,1:T(8,128)(4,1)}, u32[]{:S(2)}) copy-start(pred[8,68]{0,1:T(8,128)(4,1)} %constant.43) | copy-start | bytes 1636
  145.6 5.6 collective-permute-start.1
  147.7 4.6 collective-permute-start
  160.6 6.2 %collective-permute-start.3 = (bf16[192,15]{1,0:T(8,128)(2,1)S(1)}, bf16[192,15]{1,0:T(8,128)(2,1)S(1)}, u32[]{:S(2)}, u32[]{:S(2)}) collective-permute-start(bf16[192,15]{1,0:T(8,128)(2,1)S(1)} %get-tuple-element.30), channel_id=1, source_target_pairs={{8,0},{16,8},{24,16},{32,24},{40,32},{48,40},{56,48},{64,56},{72,6... | collective-permute-start | bytes 17288 | tf_op jit(solution)/shard_map/ppermute | solution.py:17
  162.5 5.4 collective-permute-start.2
  178.1 4.3 copy-start.1
  178.1 303.6 %all-reduce.4.cloned.1.call-start = ((), (), s32[]{:S(2)}) async-start(), calls=%async_computation.5 | async-start | bytes 4718592
  228.9 355.8 %all-to-all-start = ((bf16[8,192,64]{1,2,0:T(8,128)(2,1)}), bf16[8,192,64]{1,2,0:T(8,128)(2,1)S(1)}, u32[]{:S(2)}, u32[]{:S(2)}) async-start(bf16[8,192,64]{1,2,0:T(8,128)(2,1)} %copy.54), calls=%async_computation.1 | async-start | bytes 524288 | tf_op jit(solution)/shard_map/all_to_all | solution.py:116
Sparse Core Ops, SparseCore 0:
  10.1 45.0 all-gather.4
  59.0 84.0 all-gather.2
  178.3 47.0 reduce-scatter.1
  228.6 202.0 all-reduce.3
where the time goes:
time: 593 us; the launch traced here: 592 us
  blocking collectives  367 us (62%)
  waiting for transfers between devices  150 us (25%)
  starting transfers between devices  16.8 us (3%)
  local copies, waits for them, and re-layouts  16.6 us (3%)
  between operations  15.3 us (3%)
  matrix products  14.7 us (2%)
  other arithmetic  11.8 us (2%)
    psum x1, blocking collectives, shards(): grad_taps = lax.psum(tap_partial, 'seq')  246 us
    psum x1, blocking collectives, shards(): gain_whole = lax.psum(gain_portion, ('seq', 'ch'))  101 us
    all_gather x1, waiting for transfers between devices, shards(): gathered = lax.all_gather(stacked, 'seq', axis=0, tiled=True)  85.3 us
    reduce_scatter x1, waiting for transfers between devices, shards(): lax.psum_scatter(normed_term.astype(jnp.bfloat16), 'ch', scatter_dimensio...  38.9 us
    all_gather x1, waiting for transfers between devices, shards(): lax.all_gather(signal, 'ch', axis=0, tiled=True)  22.6 us
    unnamed x1, blocking collectives  20.2 us
  transfers between devices with their start and end apart: 9, of which 5 were waited for; matrix products, arithmetic and copies ran while one was open for 4% of the time, Pallas kernels for 0%

commit v1 on v0

--- a/solution.py
+++ b/solution.py
@@ -2,6 +2,19 @@
 import jax.numpy as jnp
 from jax import lax
 from jax.sharding import PartitionSpec as P
+
+
+def collect(x, axis, dim):
+    ways = lax.axis_size(axis)
+    up = [(d, (d + 1) % ways) for d in range(ways)]
+    down = [(d, (d - 1) % ways) for d in range(ways)]
+    earlier, later = ([x], [x])
+    for _ in range(ways // 2):
+        earlier.append(lax.ppermute(earlier[-1], axis, up))
+    for _ in range((ways - 1) // 2):
+        later.append(lax.ppermute(later[-1], axis, down))
+    line = jnp.concatenate([*earlier[::-1], *later[1:]], axis=dim)
+    return jnp.roll(line, (lax.axis_index(axis) - ways // 2) * x.shape[dim], axis=dim)
 
 
 def extended(cells, sides, width):
@@ -52,7 +65,7 @@
     channel_position = lax.axis_index("ch")
     reach = depth_taps.shape[0] // 2
     complete_signal, complete_gain = (
-        lax.all_gather(signal, "ch", axis=0, tiled=True),
+        collect(signal, "ch", 0),
         lax.all_gather(input_norm_gain.astype(jnp.bfloat16), "ch", axis=0, tiled=True).astype(
             input_norm_gain.dtype
         ),

time: 593 us -> 564 us (0.951)
  waiting for transfers between devices: 150 us -> 72.6 us
  starting transfers between devices: 16.8 us -> 45 us
  local copies, waits for them, and re-layouts: 16.6 us -> 36.5 us
  blocking collectives: 367 us -> 360 us
    all_gather x1, waiting for transfers between devices: 85.3 us -> 26.2 us  [shards(): gathered = lax.all_gather(stacked, 'seq', axis=0, tiled=True)]
    ppermute x0 -> x7, starting transfers between devices: none -> 28.3 us  [the longest x3 17.7 us: collect(): later.append(lax.ppermute(later[-1], axis, down))]
    all_gather x1 -> x0, waiting for transfers between devices: 22.6 us -> none  [shards(): lax.all_gather(signal, 'ch', axis=0, tiled=True)]
    conv_general_dilated x10, local copies, waits for them, and re-layouts: 6.57 us -> 16.6 us  [depthwise(): lax.conv_general_dilated(padded[None], kernel, (1,), 'VALID', dimension_n...]
    ppermute x0 -> x7, waiting for transfers between devices: none -> 9.45 us  [the longest x4 9.44 us: collect(): earlier.append(lax.ppermute(earlier[-1], axis, up))]
    unnamed x1, blocking collectives: 20.2 us -> 13.6 us
  transfers between devices with their start and end apart: 9 -> 15, of which waited for: 5 -> 7; matrix products, arithmetic and copies ran while one was open for 4% -> 6% of each run, Pallas kernels for 0% -> 0%
where the time goes in v1:
time: 564 us; the launch traced here: 562 us
  blocking collectives  360 us (64%)
  waiting for transfers between devices  72.6 us (13%)
  starting transfers between devices  45 us (8%)
  local copies, waits for them, and re-layouts  36.5 us (6%)
  matrix products  18 us (3%)
  between operations  15.5 us (3%)
  other arithmetic  14.7 us (3%)
    psum x1, blocking collectives, shards(): grad_taps = lax.psum(tap_partial, 'seq')  246 us
    psum x1, blocking collectives, shards(): gain_whole = lax.psum(gain_portion, ('seq', 'ch'))  101 us
    reduce_scatter x1, waiting for transfers between devices, shards(): lax.psum_scatter(normed_term.astype(jnp.bfloat16), 'ch', scatter_dimensio...  34.8 us
    all_gather x1, waiting for transfers between devices, shards(): gathered = lax.all_gather(stacked, 'seq', axis=0, tiled=True)  26.2 us
    ppermute x3, starting transfers between devices, collect(): later.append(lax.ppermute(later[-1], axis, down))  17.7 us
    conv_general_dilated x10, local copies, waits for them, and re-layouts, depthwise(): lax.conv_general_dilated(padded[None], kernel, (1,), 'VALID', dimension_n...  16.6 us
    unnamed x1, blocking collectives  13.6 us
  transfers between devices with their start and end apart: 15, of which 7 were waited for; matrix products, arithmetic and copies ran while one was open for 6% of the time, Pallas kernels for 0%

profile of v1, /device:TPU:1, one launch (start us, length us, event | category | flops | bytes accessed | tf_op | source)
XLA Modules:
  0.0 562.3 jit_solution(11069177538668482787)
XLA Ops:
  7.2 1.4 pad_maximum_fusion.4
  9.8 4.8 collective-permute-start
  14.6 8.6 %collective-permute-start.4 = (bf16[192,512]{0,1:T(8,128)(2,1)S(1)}, bf16[192,512]{0,1:T(8,128)(2,1)S(1)}, u32[]{:S(2)}, u32[]{:S(2)}) collective-permute-start(bf16[192,512]{0,1:T(8,128)(2,1)S(1)} %copy.47), channel_id=1, source_target_pairs={{0,7},{1,0},{2,1},{3,2},{4,3},{5,4},{6,5},{7,6},{8,15},{9,8},{10,9... | collective-permute-start | bytes 589832 | tf_op jit(solution)/shard_map/ppermute | solution.py:15
  23.2 4.1 collective-permute-done
  27.3 1.9 collective-permute-start.1
  29.2 4.6 collective-permute-start.5
  33.8 3.1 collective-permute-done.1
  37.0 1.9 collective-permute-start.2
  38.9 4.6 collective-permute-start.6
  43.5 2.2 collective-permute-done.2
  45.7 1.9 collective-permute-start.3
  48.3 1.3 dynamic-slice.4
  50.5 13.6 %all-reduce = bf16[1536]{0:T(1024)(128)(2,1)S(1)} all-reduce(bf16[1536]{0:T(1024)(128)(2,1)S(1)} %dynamic-update-slice), channel_id=1, replica_groups=mesh['seq'=64,'ch'=8] {'ch'}, use_global_device_ids=true, to_apply=%add | all-reduce | flops 1536 | bytes 6144
  64.9 5.5 concatenate.19
  70.5 1.2 convert_reduce_fusion
  71.7 1.5 fusion.2
  73.2 26.2 %all-gather.2.cloned.1.call-done = bf16[1536,384]{1,0:T(8,128)(2,1)} async-done(((bf16[24,384]{1,0:T(8,128)(2,1)}), bf16[1536,384]{1,0:T(8,128)(2,1)}) %all-gather.2.cloned.1.call-update) | async-done | bytes 1179664 | tf_op jit(solution)/shard_map/all_gather | solution.py:82
  99.4 2.9 fusion.6
  103.4 2.1 collective-permute-start.8
  105.5 3.4 collective-permute-start.7
  109.0 1.1 collective-permute-done.7
  111.0 1.1 reshape.83
  112.1 1.4 copy.53
  113.6 2.0 convolution_select_fusion.1
  115.7 2.3 copy.67
  117.9 2.2 reshape.80
  120.1 2.0 multiply_convert_fusion.5
  122.1 1.9 collective-permute-start.10
  124.1 4.4 collective-permute-start.9
  130.4 2.1 reshape.84
  132.4 2.1 copy.59
  135.5 3.0 convolution_select_fusion
  138.5 2.3 copy.68
  140.8 2.2 reshape.81
  142.9 1.4 multiply_convert_fusion.4
  145.1 3.6 convolution_convert_fusion
  148.7 1.3 dynamic-slice.5
  150.7 2.9 fusion
  153.6 2.1 copy.64
  156.8 4.3 fusion.5
  161.1 34.8 %reduce-scatter.2.cloned.1.call-done = bf16[1536,64]{0,1:T(8,128)(2,1)} async-done(((bf16[1536,512]{0,1:T(8,128)(2,1)}), bf16[1536,64]{0,1:T(8,128)(2,1)}) %reduce-scatter.2.cloned.1.call-update) | async-done | bytes 196624 | tf_op jit(solution)/shard_map/reduce_scatter | solution.py:120
  195.9 1.3 fusion.26
  197.2 1.2 fusion.24
  199.5 4.7 all-to-all-start
  204.2 2.2 fusion.49
  206.4 245.8 %psum.14 = f32[31,192]{1,0:T(8,128)} all-reduce(f32[31,192]{1,0:T(8,128)S(1)} %bitcast.60), channel_id=1, replica_groups=mesh['seq'=64,'ch'=8] {'seq'}, use_global_device_ids=true, to_apply=%region_6.7 | all-reduce | flops 5952 | bytes 47616 | tf_op jit(solution)/shard_map/psum | solution.py:102
  452.2 1.5 fusion.46
  453.7 100.6 %psum.15 = f32[1536]{0:T(1024)S(1)} all-reduce(f32[1536]{0:T(1024)S(1)} %get-tuple-element.18), channel_id=1, replica_groups=mesh['seq'=64,'ch'=8] {'seq','ch'}, use_global_device_ids=true, to_apply=%region_8.9 | all-reduce | flops 1536 | bytes 12288 | tf_op jit(solution)/shard_map/psum | solution.py:131
  (65 shorter events, 12.1 us)
Async XLA Ops:
  7.2 106.4 %copy-start = (f32[31,192]{1,0:T(8,128)S(1)}, f32[31,192]{1,0:T(8,128)}, u32[]{:S(2)}) copy-start(f32[31,192]{1,0:T(8,128)} %param.10) | copy-start | bytes 71428
  7.2 92.2 %all-gather.2.cloned.1.call-start = ((), (), s32[]{:S(2)}) async-start(), calls=%async_computation.2 | async-start | bytes 1198080 | tf_op jit(solution)/shard_map/all_gather | solution.py:82
  8.7 187.2 %reduce-scatter.2.cloned.1.call-start = ((), (), s32[]{:S(2)}) async-start(), calls=%async_computation.3 | async-start | bytes 1769472 | tf_op jit(solution)/shard_map/reduce_scatter | solution.py:120
  9.8 17.5 %collective-permute-start = (bf16[192,512]{0,1:T(8,128)(2,1)S(1)}, bf16[192,512]{0,1:T(8,128)(2,1)S(1)}, u32[]{:S(2)}, u32[]{:S(2)}) collective-permute-start(bf16[192,512]{0,1:T(8,128)(2,1)S(1)} %copy.47), channel_id=1, source_target_pairs={{0,1},{1,2},{2,3},{3,4},{4,5},{5,6},{6,7},{7,0},{8,9},{9,10},{10,1... | collective-permute-start | bytes 589832 | tf_op jit(solution)/shard_map/ppermute | solution.py:13
  14.6 14.6 %collective-permute-start.4 = (bf16[192,512]{0,1:T(8,128)(2,1)S(1)}, bf16[192,512]{0,1:T(8,128)(2,1)S(1)}, u32[]{:S(2)}, u32[]{:S(2)}) collective-permute-start(bf16[192,512]{0,1:T(8,128)(2,1)S(1)} %copy.47), channel_id=1, source_target_pairs={{0,7},{1,0},{2,1},{3,2},{4,3},{5,4},{6,5},{7,6},{8,15},{9,8},{10,9... | collective-permute-start | bytes 589832 | tf_op jit(solution)/shard_map/ppermute | solution.py:15
  27.3 1.9 copy-start.2
  27.3 9.7 %collective-permute-start.1 = (bf16[192,512]{0,1:T(8,128)(2,1)S(1)}, bf16[192,512]{0,1:T(8,128)(2,1)S(1)}, u32[]{:S(2)}, u32[]{:S(2)}) collective-permute-start(bf16[192,512]{0,1:T(8,128)(2,1)S(1)} %collective-permute-done), channel_id=1, source_target_pairs={{0,1},{1,2},{2,3},{3,4},{4,5},{5,6},{6,7},{7,0},{8,9},{9,10},{10,1... | collective-permute-start | bytes 589832 | tf_op jit(solution)/shard_map/ppermute | solution.py:13
  29.2 7.7 %copy-start.3 = (bf16[192,512]{0,1:T(8,128)(2,1)}, bf16[192,512]{0,1:T(8,128)(2,1)S(1)}, u32[]{:S(2)}) copy-start(bf16[192,512]{0,1:T(8,128)(2,1)S(1)} %collective-permute-done.4) | copy-start | bytes 589828
  29.2 9.6 %collective-permute-start.5 = (bf16[192,512]{0,1:T(8,128)(2,1)S(1)}, bf16[192,512]{0,1:T(8,128)(2,1)S(1)}, u32[]{:S(2)}, u32[]{:S(2)}) collective-permute-start(bf16[192,512]{0,1:T(8,128)(2,1)S(1)} %collective-permute-done.4), channel_id=1, source_target_pairs={{0,7},{1,0},{2,1},{3,2},{4,3},{5,4},{6,5},{7,6},{8,15},{9,8},{10,9... | collective-permute-start | bytes 589832 | tf_op jit(solution)/shard_map/ppermute | solution.py:15
  37.0 1.9 copy-start.4
  37.0 8.7 %collective-permute-start.2 = (bf16[192,512]{0,1:T(8,128)(2,1)S(1)}, bf16[192,512]{0,1:T(8,128)(2,1)S(1)}, u32[]{:S(2)}, u32[]{:S(2)}) collective-permute-start(bf16[192,512]{0,1:T(8,128)(2,1)S(1)} %collective-permute-done.1), channel_id=1, source_target_pairs={{0,1},{1,2},{2,3},{3,4},{4,5},{5,6},{6,7},{7,0},{8,9},{9,10},{10,1... | collective-permute-start | bytes 589832 | tf_op jit(solution)/shard_map/ppermute | solution.py:13
  38.9 25.3 %copy-start.5 = (bf16[192,512]{0,1:T(8,128)(2,1)}, bf16[192,512]{0,1:T(8,128)(2,1)S(1)}, u32[]{:S(2)}) copy-start(bf16[192,512]{0,1:T(8,128)(2,1)S(1)} %collective-permute-done.5) | copy-start | bytes 589828
  38.9 25.3 %collective-permute-start.6 = (bf16[192,512]{0,1:T(8,128)(2,1)S(1)}, bf16[192,512]{0,1:T(8,128)(2,1)S(1)}, u32[]{:S(2)}, u32[]{:S(2)}) collective-permute-start(bf16[192,512]{0,1:T(8,128)(2,1)S(1)} %collective-permute-done.5), channel_id=1, source_target_pairs={{0,7},{1,0},{2,1},{3,2},{4,3},{5,4},{6,5},{7,6},{8,15},{9,8},{10,9... | collective-permute-start | bytes 589832 | tf_op jit(solution)/shard_map/ppermute | solution.py:15
  45.7 18.5 %copy-start.6 = (bf16[192,512]{0,1:T(8,128)(2,1)}, bf16[192,512]{0,1:T(8,128)(2,1)S(1)}, u32[]{:S(2)}) copy-start(bf16[192,512]{0,1:T(8,128)(2,1)S(1)} %collective-permute-done.2) | copy-start | bytes 589828
  45.7 19.2 %collective-permute-start.3 = (bf16[192,512]{0,1:T(8,128)(2,1)S(1)}, bf16[192,512]{0,1:T(8,128)(2,1)}, u32[]{:S(2)}, u32[]{:S(2)}) collective-permute-start(bf16[192,512]{0,1:T(8,128)(2,1)S(1)} %collective-permute-done.2), channel_id=1, source_target_pairs={{0,1},{1,2},{2,3},{3,4},{4,5},{5,6},{6,7},{7,0},{8,9},{9,10},{10,1... | collective-permute-start | bytes 589832 | tf_op jit(solution)/shard_map/ppermute | solution.py:13
  64.2 0.7 copy-start.7
  102.3 0.9 copy-start.1
  103.2 10.4 %copy-start.12 = (pred[8,68]{0,1:T(8,128)(4,1)S(1)}, pred[8,68]{0,1:T(8,128)(4,1)}, u32[]{:S(2)}) copy-start(pred[8,68]{0,1:T(8,128)(4,1)} %constant.63) | copy-start | bytes 1636
  103.4 5.6 collective-permute-start.8
  105.5 4.6 collective-permute-start.7
  122.1 6.4 %collective-permute-start.10 = (bf16[192,15]{1,0:T(8,128)(2,1)S(1)}, bf16[192,15]{1,0:T(8,128)(2,1)S(1)}, u32[]{:S(2)}, u32[]{:S(2)}) collective-permute-start(bf16[192,15]{1,0:T(8,128)(2,1)S(1)} %get-tuple-element.30), channel_id=1, source_target_pairs={{8,0},{16,8},{24,16},{32,24},{40,32},{48,40},{56,48},{64,56},{72,6... | collective-permute-start | bytes 17288 | tf_op jit(solution)/shard_map/ppermute | solution.py:30
  124.1 5.4 collective-permute-start.9
  144.3 0.7 copy-start.8
  144.3 0.7 copy-start.9
  148.7 303.6 %all-reduce.4.cloned.1.call-start = ((), (), s32[]{:S(2)}) async-start(), calls=%async_computation.4 | async-start | bytes 4718592
  161.1 43.0 %copy-start.10 = (bf16[1,192,542]{1,0,2:T(2,128)(2,1)S(1)}, bf16[1,192,542]{1,0,2:T(2,128)(2,1)}, u32[]{:S(2)}) copy-start(bf16[1,192,542]{1,0,2:T(2,128)(2,1)} %copy.64) | copy-start | bytes 624388
  161.1 43.0 %copy-start.11 = (bf16[192,1,512]{0,1,2:T(2,128)(2,1)S(1)}, bf16[192,1,512]{0,1,2:T(2,128)(2,1)}, u32[]{:S(2)}) copy-start(bf16[192,1,512]{0,1,2:T(2,128)(2,1)} %copy.65) | copy-start | bytes 589828
  199.5 355.5 %all-to-all-start = ((bf16[8,192,64]{1,2,0:T(8,128)(2,1)}), bf16[8,192,64]{1,2,0:T(8,128)(2,1)S(1)}, u32[]{:S(2)}, u32[]{:S(2)}) async-start(bf16[8,192,64]{1,2,0:T(8,128)(2,1)} %copy.63), calls=%async_computation.1 | async-start | bytes 524288 | tf_op jit(solution)/shard_map/all_to_all | solution.py:129
Sparse Core Ops, SparseCore 0:
  11.9 87.4 all-gather.1
  148.8 47.0 reduce-scatter.1
  199.3 202.0 all-reduce.3
